TPU v7x, 32 devices: a whole 2x2x4 slice. The times are simulated.
32 devices in a mesh: blk: 8 (over z, x), cent: 4 (over y, core).
Axes of the slice: x: 2, y: 2, z: 4, core: 2. Of those that a mesh axis runs over, the one named last changes fastest.
Arguments:
- descriptors: bfloat16 [6144, 1024], P('blk'), may hold values from -6 to 6
- landmarks: bfloat16 [4096, 1024], P('blk'), may hold values from -6 to 6
- whitening: bfloat16 [4096, 4096], P('blk', 'cent'), may hold values from -0.09375 to 0.09375
- centroids: bfloat16 [4096, 4096], P('cent'), may hold values from -8 to 8, as said below
Outputs:
- assign: bfloat16 [6144, 4096], P('blk', 'cent')
- new_centroids: float32 [4096, 4096], P('blk', 'cent')
Inputs may be any that keep to these rules, and one draw needn't show every extreme that they name: `centroids`: centroid coordinates.
All inputs are finite; a program needn't handle non-finite values.
Results may differ from a plain program's by a relative error of at most 0.03.
Values may be sent and summed in bfloat16 or wider, within the bound.
No kernel may reach another device: no remote copies, remote signals or barrier semaphores. Data moves between devices by JAX's collectives and lax.ppermute only.
A program may use at most 128 MiB of HBM per device.

v0:
```python
import math

import jax
import jax.numpy as jnp
from jax import lax
from jax.sharding import PartitionSpec as P


def unit_rows(values):
    wide = values.astype(jnp.float32)
    sum_sq = jnp.sum(wide * wide, axis=1, keepdims=True)
    scale = lax.rsqrt(sum_sq + 1e-06)
    return (wide * scale).astype(jnp.bfloat16)


def per_device(descriptors, landmarks, whitening, centroids):
    unit_desc = unit_rows(descriptors)
    unit_land = unit_rows(landmarks)
    sharpness = math.sqrt(descriptors.shape[1])
    cosine = lax.dot_general(
        unit_desc,
        lax.all_gather(unit_land, "blk", axis=0, tiled=True),
        (((1,), (1,)), ((), ())),
        preferred_element_type=jnp.float32,
    )
    kernel = jnp.exp(sharpness * cosine).astype(jnp.bfloat16)
    feature_cols = jnp.dot(
        kernel,
        lax.all_gather(whitening, "blk", axis=0, tiled=True),
        preferred_element_type=jnp.float32,
    )
    features = lax.all_gather(feature_cols.astype(jnp.bfloat16), "cent", axis=1, tiled=True)
    logits = lax.dot_general(
        features, centroids, (((1,), (1,)), ((), ())), preferred_element_type=jnp.float32
    )
    local_top = jnp.max(logits, axis=1)
    row_top = lax.pmax(local_top, "cent")
    weights = jnp.exp(logits - row_top[:, None])
    row_total = lax.psum(jnp.sum(weights, axis=1), "cent")
    assign = (weights / row_total[:, None]).astype(jnp.bfloat16)
    counts = lax.psum(jnp.sum(assign.astype(jnp.float32), axis=0), "blk")
    sums = lax.psum_scatter(
        lax.dot_general(
            features, assign, (((0,), (0,)), ((), ())), preferred_element_type=jnp.float32
        ).astype(jnp.bfloat16),
        "blk",
        scatter_dimension=0,
        tiled=True,
    ).astype(jnp.float32)
    return (assign, sums / jnp.maximum(counts, 1.0)[None, :])


def solution(mesh):
    in_specs = (P("blk", None), P("blk", None), P("blk", "cent"), P("cent", None))
    out_specs = (P("blk", "cent"), P("blk", "cent"))
    return jax.shard_map(
        per_device, mesh=mesh, in_specs=in_specs, out_specs=out_specs, check_vma=False
    )
```

profile of v0, /device:TPU:0, one launch (start us, length us, event | category | flops | bytes accessed | tf_op | source)
XLA Modules:
  0.0 523.7 jit_solution(12697928453037709906)
XLA Ops:
  7.2 0.0 copy-start
  7.2 0.0 all-gather.6.cloned.1.call-start
  7.2 0.7 all-gather.6.cloned.1.call-update
  7.9 0.0 all-gather.4.cloned.1.call-start
  8.0 1.5 fusion.3
  9.5 2.4 fusion.4
  11.9 0.0 all-gather.4.cloned.1.call-update
  11.9 0.0 all-gather.8.cloned.1.call-start
  12.0 0.0 copy-done
  12.0 0.4 fusion
  12.4 125.0 %all-gather.6.cloned.1.call-done = bf16[4096,1024]{1,0:T(8,128)(2,1)} async-done(((bf16[512,1024]{1,0:T(8,128)(2,1)}), bf16[4096,1024]{1,0:T(8,128)(2,1)}) %all-gather.6.cloned.1.call-update) | async-done | bytes 8388624 | tf_op jit(solution)/shard_map/all_gather | solution.py:29
  137.3 125.4 %all-gather.4.cloned.1.call-done = bf16[4096,1024]{1,0:T(8,128)(2,1)} async-done(((bf16[512,1024]{1,0:T(8,128)(2,1)}), bf16[4096,1024]{1,0:T(8,128)(2,1)}) %all-gather.4.cloned.1.call-update) | async-done | bytes 8388624 | tf_op jit(solution)/shard_map/all_gather | solution.py:22
  262.7 20.2 %convolution_convert_fusion.1 = bf16[768,1024]{1,0:T(8,128)(2,1)} fusion(bf16[4096,1024]{1,0:T(8,128)(2,1)} %all-gather.6.cloned.1.call-done, bf16[4096,1024]{1,0:T(8,128)(2,1)} %all-gather.4.cloned.1.call-done, bf16[768,1024]{1,0:T(8,128)(2,1)S(1)} %copy-done, f32[768]{0:T(1024)S(1)} %add_rsqrt_fusion), kind=kOutput, calls=%fused_computation.15 | convolution fusion | flops 12894339072 | bytes 19926016 | tf_op jit(solution)/shard_map/dot_general | solution.py:27
  282.9 0.0 all-gather.8.cloned.1.call-update
  282.9 0.2 reduce-scatter.2.cloned.1.call-start
  283.1 44.5 %all-gather.8.cloned.1.call-done = bf16[768,4096]{1,0:T(8,128)(2,1)} async-done(((bf16[768,1024]{1,0:T(8,128)(2,1)}), bf16[768,4096]{1,0:T(8,128)(2,1)}) %all-gather.8.cloned.1.call-update) | async-done | bytes 6291472 | tf_op jit(solution)/shard_map/all_gather | solution.py:32
  327.6 11.1 %fusion.11 = (f32[768]{0:T(1024)S(1)}, f32[768,1024]{1,0:T(8,128)S(1)}) fusion(bf16[768,4096]{1,0:T(8,128)(2,1)} %all-gather.8.cloned.1.call-done, bf16[1024,4096]{1,0:T(8,128)(2,1)} %param.7), kind=kOutput, calls=%fused_computation.21 | convolution fusion | flops 6443236352 | bytes 17828864 | tf_op jit(solution)/shard_map/dot_general | solution.py:33
  338.7 5.9 %pmax.7 = f32[768]{0:T(1024)S(1)} all-reduce(f32[768]{0:T(1024)S(1)} %get-tuple-element.4), channel_id=1, replica_groups=mesh['blk'=8,'cent'=4] {'cent'}, use_global_device_ids=true, to_apply=%region_3.0 | all-reduce | flops 768 | bytes 6144 | tf_op jit(solution)/shard_map/pmax | solution.py:37
  344.6 0.9 fusion.2
  345.6 5.7 %psum.14 = f32[768]{0:T(1024)S(1)} all-reduce(f32[768]{0:T(1024)S(1)} %fusion.2), channel_id=1, replica_groups=mesh['blk'=8,'cent'=4] {'cent'}, use_global_device_ids=true, to_apply=%region_5.0 | all-reduce | flops 768 | bytes 6144 | tf_op jit(solution)/shard_map/psum | solution.py:39
  351.2 1.0 convert_reduce_fusion
  352.2 0.0 copy-start.1
  352.2 1.1 copy-done.1
  353.4 11.9 %convolution_convert_fusion = bf16[4096,1024]{1,0:T(8,128)(2,1)} fusion(bf16[768,4096]{1,0:T(8,128)(2,1)} %all-gather.8.cloned.1.call-done, bf16[768,1024]{1,0:T(8,128)(2,1)S(1)} %get-tuple-element.3), kind=kOutput, calls=%fused_computation.1 | convolution fusion | flops 6446645248 | bytes 16252928 | tf_op jit(solution)/shard_map/dot_general | solution.py:43
  365.2 0.0 reduce-scatter.2.cloned.1.call-update
  365.3 22.1 %psum.15 = f32[1024]{0:T(1024)S(1)} all-reduce(f32[1024]{0:T(1024)S(1)} %get-tuple-element.2), channel_id=1, replica_groups=mesh['blk'=8,'cent'=4] {'blk'}, use_global_device_ids=true, to_apply=%region_8.0 | all-reduce | flops 1024 | bytes 8192 | tf_op jit(solution)/shard_map/psum | solution.py:41
  387.4 127.0 %reduce-scatter.2.cloned.1.call-done = bf16[512,1024]{1,0:T(8,128)(2,1)} async-done(((bf16[4096,1024]{1,0:T(8,128)(2,1)}), bf16[512,1024]{1,0:T(8,128)(2,1)}) %reduce-scatter.2.cloned.1.call-update) | async-done | bytes 1048592 | tf_op jit(solution)/shard_map/reduce_scatter | solution.py:42
  514.3 2.9 convert_divide_fusion
  (3 shorter events, 0.0 us)
Async XLA Ops:
  7.2 4.8 copy-start
  7.2 130.2 %all-gather.6.cloned.1.call-start = ((), (), s32[]{:S(2)}) async-start(), calls=%async_computation.2 | async-start | bytes 9437184 | tf_op jit(solution)/shard_map/all_gather | solution.py:29
  7.9 254.8 %all-gather.4.cloned.1.call-start = ((), (), s32[]{:S(2)}) async-start(), calls=%async_computation.1 | async-start | bytes 9437184 | tf_op jit(solution)/shard_map/all_gather | solution.py:22
  11.9 315.7 %all-gather.8.cloned.1.call-start = ((), (), s32[]{:S(2)}) async-start(), calls=%async_computation.3 | async-start | bytes 7864320 | tf_op jit(solution)/shard_map/all_gather | solution.py:32
  282.9 231.4 %reduce-scatter.2.cloned.1.call-start = ((), (), s32[]{:S(2)}) async-start(), calls=%async_computation.4 | async-start | bytes 9437184 | tf_op jit(solution)/shard_map/reduce_scatter | solution.py:42
  352.2 1.1 copy-start.1
Sparse Core Ops, SparseCore 0:
  10.1 127.1 all-gather.5
  140.0 122.6 all-gather.3
  283.0 44.5 all-gather.7
  365.4 148.9 reduce-scatter.1
where the time goes:
time: 524 us
  waiting for transfers between devices  423 us (81%)
  matrix products  43.2 us (8%)
  blocking collectives  33.7 us (6%)
  between operations  13.8 us (3%)
  other arithmetic  9.08 us (2%)
    reduce_scatter x1, waiting for transfers between devices, per_device(): lax.psum_scatter(lax.dot_general(features, assign, (((0,), (0,)), ((), ()...  127 us
    all_gather x1, waiting for transfers between devices, per_device(): lax.all_gather(unit_land, 'blk', axis=0, tiled=True)  125 us
    all_gather x1, waiting for transfers between devices, per_device(): lax.all_gather(whitening, 'blk', axis=0, tiled=True)  125 us
    all_gather x1, waiting for transfers between devices, per_device(): lax.all_gather(feature_cols.astype(jnp.bfloat16), 'cent', axis=1, tiled=T...  44.5 us
    psum x1, blocking collectives, per_device(): counts = lax.psum(jnp.sum(assign.astype(jnp.float32), axis=0), 'blk')  22.1 us
    dot_general x1, matrix products, per_device(): jnp.dot(kernel, lax.all_gather(whitening, 'blk', axis=0, tiled=True), pre...  20.2 us
    dot_general x1, matrix products, per_device(): lax.dot_general(features, assign, (((0,), (0,)), ((), ())), preferred_ele...  11.9 us
    dot_general x1, matrix products, per_device(): lax.dot_general(features, centroids, (((1,), (1,)), ((), ())), preferred_...  11.1 us
  transfers between devices with their start and end apart: 4, of which 4 were waited for; matrix products, arithmetic and copies ran while one was open for 1% of the time, Pallas kernels for 0%

commit v1 on v0

v1 whole, which is shorter than its diff:
```python
import math

import jax
import jax.numpy as jnp
from jax import lax
from jax.sharding import PartitionSpec as P


def unit_rows(values):
    wide = values.astype(jnp.float32)
    sum_sq = jnp.sum(wide * wide, axis=1, keepdims=True)
    scale = lax.rsqrt(sum_sq + 1e-06)
    return (wide * scale).astype(jnp.bfloat16)


def ring_order(nb):
    if nb % 2:
        return list(range(nb))
    half = nb // 2
    return [2 * i for i in range(half)] + [2 * i + 1 for i in reversed(range(half))]


def make_per_device(nb, nc):
    ring = ring_order(nb)
    pos_of = [0] * nb
    for i, b in enumerate(ring):
        pos_of[b] = i
    fwd = [(ring[i], ring[(i + 1) % nb]) for i in range(nb)]
    bwd = [(ring[(i + 1) % nb], ring[i]) for i in range(nb)]
    ring_arr = jnp.array(ring, jnp.int32)
    pos_arr = jnp.array(pos_of, jnp.int32)

    def per_device(descriptors, landmarks, whitening, centroids):
        me = lax.axis_index("blk")
        cme = lax.axis_index("cent")
        p = pos_arr[me]

        def ring_blk(i):
            return ring_arr[i % nb]

        unit_desc = unit_rows(descriptors)
        unit_land = unit_rows(landmarks)
        ml = unit_land.shape[0]
        q = ml // nc
        quarter = lax.dynamic_slice_in_dim(unit_land, cme * q, q, axis=0)
        lq = lax.all_gather(quarter, "blk", axis=0, tiled=False)
        lall = lax.all_gather(lq, "cent", axis=0, tiled=False)
        land_full = jnp.transpose(lall, (1, 0, 2, 3)).reshape(nb * ml, -1)

        sharpness = math.sqrt(descriptors.shape[1])
        cosine = lax.dot_general(
            unit_desc, land_full, (((1,), (1,)), ((), ())), preferred_element_type=jnp.float32
        )
        kernel = jnp.exp(sharpness * cosine).astype(jnp.bfloat16)

        mw = whitening.shape[0]
        h = mw // 2

        def kcols(blk, off):
            return lax.dynamic_slice_in_dim(kernel, blk * mw + off, h, axis=1)

        wa = whitening[:h]
        wb = whitening[h:]
        acc = jnp.dot(kcols(me, 0), wa, preferred_element_type=jnp.float32)
        acc = acc + jnp.dot(kcols(me, h), wb, preferred_element_type=jnp.float32)

        def w_step(s, carry):
            wa, wb, acc = carry
            na = lax.ppermute(wa, "blk", fwd)
            nbk = lax.ppermute(wb, "blk", bwd)
            if s is not None:
                acc = acc + jnp.dot(kcols(ring_blk(p - s), 0), wa, preferred_element_type=jnp.float32)
                acc = acc + jnp.dot(kcols(ring_blk(p + s), h), wb, preferred_element_type=jnp.float32)
            return na, nbk, acc

        wa, wb, _ = w_step(None, (wa, wb, acc))
        wa, wb, acc = lax.fori_loop(1, nb - 1, w_step, (wa, wb, acc))
        s_last = nb - 1
        acc = acc + jnp.dot(kcols(ring_blk(p - s_last), 0), wa, preferred_element_type=jnp.float32)
        acc = acc + jnp.dot(kcols(ring_blk(p + s_last), h), wb, preferred_element_type=jnp.float32)
        feature_cols = acc.astype(jnp.bfloat16)

        features = lax.all_gather(feature_cols, "cent", axis=1, tiled=True)
        logits = lax.dot_general(
            features, centroids, (((1,), (1,)), ((), ())), preferred_element_type=jnp.float32
        )
        local_top = jnp.max(logits, axis=1)
        row_top = lax.pmax(local_top, "cent")
        weights = jnp.exp(logits - row_top[:, None])
        row_total = lax.psum(jnp.sum(weights, axis=1), "cent")
        assign = (weights / row_total[:, None]).astype(jnp.bfloat16)
        part_counts = jnp.sum(assign.astype(jnp.float32), axis=0)
        counts = jnp.sum(lax.all_gather(part_counts, "blk", axis=0, tiled=False), axis=0)

        rb = features.shape[1] // nb
        rh = rb // 2

        def part_sums(blk, off):
            cols = lax.dynamic_slice_in_dim(features, blk * rb + off, rh, axis=1)
            return lax.dot_general(
                cols, assign, (((0,), (0,)), ((), ())), preferred_element_type=jnp.float32
            )

        def r_step(s, carry):
            acc_a, acc_b = carry
            ra = lax.ppermute(acc_a.astype(jnp.bfloat16), "blk", fwd)
            rbk = lax.ppermute(acc_b.astype(jnp.bfloat16), "blk", bwd)
            acc_a = ra.astype(jnp.float32) + part_sums(ring_blk(p - 1 - s), 0)
            acc_b = rbk.astype(jnp.float32) + part_sums(ring_blk(p + 1 + s), rh)
            return acc_a, acc_b

        acc_a = part_sums(ring_blk(p - 1), 0)
        acc_b = part_sums(ring_blk(p + 1), rh)
        acc_a, acc_b = lax.fori_loop(1, nb, r_step, (acc_a, acc_b))
        sums = jnp.concatenate([acc_a, acc_b], axis=0)
        return (assign, sums / jnp.maximum(counts, 1.0)[None, :])

    return per_device


def solution(mesh):
    in_specs = (P("blk", None), P("blk", None), P("blk", "cent"), P("cent", None))
    out_specs = (P("blk", "cent"), P("blk", "cent"))
    per_device = make_per_device(mesh.shape["blk"], mesh.shape["cent"])
    return jax.shard_map(
        per_device, mesh=mesh, in_specs=in_specs, out_specs=out_specs, check_vma=False
    )
```

time: 524 us -> 491 us (0.937)
  waiting for transfers between devices: 423 us -> 196 us
  matrix products: 43.2 us -> 103 us
  local copies, waits for them, and re-layouts: 1.14 us -> 47 us
  starting transfers between devices: 0.34 us -> 29.1 us
  loops' own time: 0 us -> 24.5 us
  other arithmetic: 9.08 us -> 26.3 us
  blocking collectives: 33.7 us -> 42.4 us
  between operations: 13.8 us -> 19.1 us
    all_gather x3, waiting for transfers between devices: 295 us -> 144 us  [the longest x1 51.9 us: per_device(): lq = lax.all_gather(quarter, 'blk', axis=0, tiled=False)]
    reduce_scatter x1 -> x0, waiting for transfers between devices: 127 us -> none  [per_device(): lax.psum_scatter(lax.dot_general(features, assign, (((0,), (0,)), ((), ()...]
    dot_general x2 -> x33, matrix products: 32 us -> 92.3 us  [the longest x16 35.8 us: part_sums(): lax.dot_general(cols, assign, (((0,), (0,)), ((), ())), preferred_element...]
    ppermute x0 -> x28, waiting for transfers between devices: none -> 52.8 us  [the longest x7 41.4 us: r_step(): rbk = lax.ppermute(acc_b.astype(jnp.bfloat16), 'blk', bwd)]
    all_gather x0 -> x1, blocking collectives: none -> 30.8 us  [per_device(): lax.all_gather(part_counts, 'blk', axis=0, tiled=False)]
    ppermute x0 -> x28, starting transfers between devices: none -> 29 us  [the longest x7 8.96 us: w_step(): na = lax.ppermute(wa, 'blk', fwd)]
    while x0 -> x26, local copies, waits for them, and re-layouts: none -> 28 us
    another operation x0 -> x2, loops' own time: none -> 24.5 us  [the longest x1 15.4 us: per_device(): wa, wb, acc = lax.fori_loop(1, nb - 1, w_step, (wa, wb, acc))]
  transfers between devices with their start and end apart: 4 -> 31, of which waited for: 4 -> 19; matrix products, arithmetic and copies ran while one was open for 1% -> 21% of each run, Pallas kernels for 0% -> 0%
where the time goes in v1:
time: 491 us; the launch traced here: 488 us
  waiting for transfers between devices  196 us (40%)
  matrix products  103 us (21%)
  local copies, waits for them, and re-layouts  47 us (10%)
  blocking collectives  42.4 us (9%)
  starting transfers between devices  29.1 us (6%)
  other arithmetic  26.3 us (5%)
  loops' own time  24.5 us (5%)
  between operations  19.1 us (4%)
    all_gather x1, waiting for transfers between devices, per_device(): lq = lax.all_gather(quarter, 'blk', axis=0, tiled=False)  51.9 us
    all_gather x1, waiting for transfers between devices, per_device(): lall = lax.all_gather(lq, 'cent', axis=0, tiled=False)  49.9 us
    all_gather x1, waiting for transfers between devices, per_device(): features = lax.all_gather(feature_cols, 'cent', axis=1, tiled=True)  41.8 us
    ppermute x7, waiting for transfers between devices, r_step(): rbk = lax.ppermute(acc_b.astype(jnp.bfloat16), 'blk', bwd)  41.4 us
    dot_general x16, matrix products, part_sums(): lax.dot_general(cols, assign, (((0,), (0,)), ((), ())), preferred_element...  35.8 us
    all_gather x1, blocking collectives, per_device(): lax.all_gather(part_counts, 'blk', axis=0, tiled=False)  30.8 us
    while x26, local copies, waits for them, and re-layouts  28 us
    dot_general x6, matrix products, w_step(): jnp.dot(kcols(ring_blk(p + s), h), wb, preferred_element_type=jnp.float32)  26.9 us
  transfers between devices with their start and end apart: 31, of which 19 were waited for; matrix products, arithmetic and copies ran while one was open for 21% of the time, Pallas kernels for 0%

profile of v1, /device:TPU:0, one launch (start us, length us, event | category | flops | bytes accessed | tf_op | source)
XLA Modules:
  0.0 488.3 jit_solution(18402103548160448527)
XLA Ops:
  11.3 51.9 %all-gather.9.cloned.1.call-done = bf16[1024,1024]{1,0:T(8,128)(2,1)} async-done(((bf16[128,1024]{1,0:T(8,128)(2,1)}), bf16[1024,1024]{1,0:T(8,128)(2,1)}) %all-gather.9.cloned.1.call-update) | async-done | bytes 2097168 | tf_op jit(solution)/shard_map/all_gather | solution.py:46
  71.7 49.9 %all-gather.11.cloned.1.call-done = bf16[32,128,1024]{2,1,0:T(8,128)(2,1)} async-done(((bf16[8,128,1024]{2,1,0:T(8,128)(2,1)}), bf16[32,128,1024]{2,1,0:T(8,128)(2,1)}) %all-gather.11.cloned.1.call-update) | async-done | bytes 8388624 | tf_op jit(solution)/shard_map/all_gather | solution.py:47
  121.6 8.2 %copy.10 = bf16[8,4,128,1024]{3,2,1,0:T(8,128)(2,1)} copy(bf16[8,4,128,1024]{3,2,0,1:T(8,128)(2,1)} %bitcast.49) | data formatting | bytes 16777216 | tf_op jit(solution)/shard_map/transpose | solution.py:48
  129.8 10.9 %exponential_convert_fusion = bf16[768,4096]{1,0:T(8,128)(2,1)S(1)} fusion(bf16[4096,1024]{1,0:T(8,128)(2,1)} %bitcast.50, bf16[768,1024]{1,0:T(8,128)(2,1)S(1)} %copy-done.6, f32[768]{0:T(1024)S(1)} %add_rsqrt_fusion), kind=kOutput, calls=%fused_computation.14 | convolution fusion | flops 6451101696 | bytes 16256000 | tf_op jit(solution)/shard_map/dot_general | solution.py:51
  141.4 2.8 convolution_add_fusion
  144.4 100.9 %while.38 = (s32[]{:T(128)}, bf16[256,1024]{1,0:T(8,128)(2,1)}, bf16[256,1024]{1,0:T(8,128)(2,1)}, f32[768,1024]{1,0:T(8,128)}, s32[]{:T(128)}, /*index=5*/bf16[...) while((s32[]{:T(128)}, bf16[256,1024]{1,0:T(8,128)(2,1)}, ...), condition=%wide.region_3.4_spmd.clone, body=%wide.region_2.3_spmd.sunk.clone.sunk | while | flops 806879232 | bytes 20710044 | solution.py:77
  155.1 4.5 add_add_fusion.2
  160.7 3.1 collective-permute-done.1
  174.4 4.5 add_add_fusion.2
  178.9 3.0 collective-permute-done.1
  192.7 4.5 add_add_fusion.2
  209.8 4.5 add_add_fusion.2
  225.6 4.5 add_add_fusion.2
  240.8 4.5 add_add_fusion.2
  247.5 3.0 add_convert_fusion
  251.7 41.8 %all-gather.7.cloned.1.call-done = bf16[768,4096]{1,0:T(8,128)(2,1)} async-done(((bf16[768,1024]{1,0:T(8,128)(2,1)}), bf16[768,4096]{1,0:T(8,128)(2,1)}) %all-gather.7.cloned.1.call-update) | async-done | bytes 6291472 | tf_op jit(solution)/shard_map/all_gather | solution.py:83
  293.5 11.1 %fusion.46 = (f32[768]{0:T(1024)S(1)}, f32[768,1024]{1,0:T(8,128)S(1)}) fusion(bf16[768,4096]{1,0:T(8,128)(2,1)} %all-gather.7.cloned.1.call-done, bf16[1024,4096]{1,0:T(8,128)(2,1)} %param.13), kind=kOutput, calls=%fused_computation.56 | convolution fusion | flops 6443236352 | bytes 17828864 | tf_op jit(solution)/shard_map/dot_general | solution.py:84
  304.6 5.9 %pmax.7 = f32[768]{0:T(1024)S(1)} all-reduce(f32[768]{0:T(1024)S(1)} %get-tuple-element.457), channel_id=1, replica_groups=mesh['blk'=8,'cent'=4] {'cent'}, use_global_device_ids=true, to_apply=%region_5.6 | all-reduce | flops 768 | bytes 6144 | tf_op jit(solution)/shard_map/pmax | solution.py:88
  311.4 5.7 %psum.7 = f32[768]{0:T(1024)S(1)} all-reduce(f32[768]{0:T(1024)S(1)} %fusion.17), channel_id=1, replica_groups=mesh['blk'=8,'cent'=4] {'cent'}, use_global_device_ids=true, to_apply=%region_7.8 | all-reduce | flops 768 | bytes 6144 | tf_op jit(solution)/shard_map/psum | solution.py:90
  319.8 30.8 %all-gather.2 = f32[8192]{0:T(1024)S(1)} all-gather(f32[1024]{0:T(1024)S(1)} %get-tuple-element.445), channel_id=4, replica_groups=mesh['blk'=8,'cent'=4] {'blk'}, dimensions={0}, use_global_device_ids=true | all-gather | bytes 36864 | tf_op jit(solution)/shard_map/all_gather | solution.py:93
  354.8 123.6 %while.39 = (s32[]{:T(128)}, f32[256,1024]{1,0:T(8,128)}, f32[256,1024]{1,0:T(8,128)S(1)}, s32[]{:T(128)}, bf16[768,4096]{1,0:T(8,128)(2,1)}, /*index=5*/bf16[76...) while((s32[]{:T(128)}, f32[256,1024]{1,0:T(8,128)}, ...), condition=%wide.region_9.10_spmd.clone, body=%wide.region_8.9_spmd.sunk.clone.sunk | while | flops 806879232 | bytes 16515775 | solution.py:114
  361.0 4.1 collective-permute-done.3
  376.7 4.1 collective-permute-done.3
  392.4 5.2 %collective-permute-done.3 = bf16[256,1024]{1,0:T(8,128)(2,1)S(1)} collective-permute-done((bf16[256,1024]{1,0:T(8,128)(2,1)}, bf16[256,1024]{1,0:T(8,128)(2,1)S(1)}, u32[]{:S(2)}, u32[]{:S(2)}) %collective-permute-start.3) | collective-permute-done | bytes 524320 | tf_op jit(solution)/shard_map/while/body/eval_jaxpr/ppermute | solution.py:107
  409.4 6.5 %collective-permute-done.3 = bf16[256,1024]{1,0:T(8,128)(2,1)S(1)} collective-permute-done((bf16[256,1024]{1,0:T(8,128)(2,1)}, bf16[256,1024]{1,0:T(8,128)(2,1)S(1)}, u32[]{:S(2)}, u32[]{:S(2)}) %collective-permute-start.3) | collective-permute-done | bytes 524320 | tf_op jit(solution)/shard_map/while/body/eval_jaxpr/ppermute | solution.py:107
  428.7 8.3 %collective-permute-done.3 = bf16[256,1024]{1,0:T(8,128)(2,1)S(1)} collective-permute-done((bf16[256,1024]{1,0:T(8,128)(2,1)}, bf16[256,1024]{1,0:T(8,128)(2,1)S(1)}, u32[]{:S(2)}, u32[]{:S(2)}) %collective-permute-start.3) | collective-permute-done | bytes 524320 | tf_op jit(solution)/shard_map/while/body/eval_jaxpr/ppermute | solution.py:107
  439.5 2.8 convert_add_fusion.4
  448.4 9.0 %collective-permute-done.3 = bf16[256,1024]{1,0:T(8,128)(2,1)S(1)} collective-permute-done((bf16[256,1024]{1,0:T(8,128)(2,1)}, bf16[256,1024]{1,0:T(8,128)(2,1)S(1)}, u32[]{:S(2)}, u32[]{:S(2)}) %collective-permute-start.3) | collective-permute-done | bytes 524320 | tf_op jit(solution)/shard_map/while/body/eval_jaxpr/ppermute | solution.py:107
  460.0 2.8 convert_add_fusion.4
  468.9 4.1 collective-permute-done.3
  475.6 2.8 convert_add_fusion.4
  478.4 3.4 maximum_divide_fusion
  (158 shorter events, 136.6 us)
Async XLA Ops:
  7.2 56.0 %all-gather.9.cloned.1.call-start = ((), (), s32[]{:S(2)}) async-start(), calls=%async_computation.1 | async-start | bytes 2359296 | tf_op jit(solution)/shard_map/all_gather | solution.py:46
  11.2 60.1 %copy-start.6 = (bf16[768,1024]{1,0:T(8,128)(2,1)S(1)}, bf16[768,1024]{1,0:T(8,128)(2,1)}, u32[]{:S(2)}) copy-start(bf16[768,1024]{1,0:T(8,128)(2,1)} %param.10) | copy-start | bytes 4718596
  11.2 110.4 %all-gather.11.cloned.1.call-start = ((), (), s32[]{:S(2)}) async-start(), calls=%async_computation.2 | async-start | bytes 10485760 | tf_op jit(solution)/shard_map/all_gather | solution.py:47
  63.2 230.3 %all-gather.7.cloned.1.call-start = ((), (), s32[]{:S(2)}) async-start(), calls=%async_computation | async-start | bytes 7864320 | tf_op jit(solution)/shard_map/all_gather | solution.py:83
  64.1 80.3 %collective-permute-start.4 = (bf16[256,1024]{1,0:T(8,128)(2,1)}, bf16[256,1024]{1,0:T(8,128)(2,1)}, u32[]{:S(2)}, u32[]{:S(2)}) collective-permute-start(bf16[256,1024]{1,0:T(8,128)(2,1)} %get-tuple-element.452), channel_id=1, source_target_pairs={{0,8},{8,16},{16,24},{24,28},{28,20},{20,12},{12,4},{4,0},{1,9},{9... | collective-permute-start | bytes 1572872 | tf_op jit(solution)/shard_map/ppermute | solution.py:69
  65.7 78.7 %collective-permute-start.5 = (bf16[256,1024]{1,0:T(8,128)(2,1)S(1)}, bf16[256,1024]{1,0:T(8,128)(2,1)}, u32[]{:S(2)}, u32[]{:S(2)}) collective-permute-start(bf16[256,1024]{1,0:T(8,128)(2,1)S(1)} %get-tuple-element.451), channel_id=1, source_target_pairs={{8,0},{16,8},{24,16},{28,24},{20,28},{12,20},{4,12},{0,4},{9,1},{1... | collective-permute-start | bytes 1572872 | tf_op jit(solution)/shard_map/ppermute | solution.py:70
  146.3 14.4 %collective-permute-start = (bf16[256,1024]{1,0:T(8,128)(2,1)}, bf16[256,1024]{1,0:T(8,128)(2,1)}, u32[]{:S(2)}, u32[]{:S(2)}) collective-permute-start(bf16[256,1024]{1,0:T(8,128)(2,1)} %copy.16), channel_id=1, source_target_pairs={{0,8},{8,16},{16,24},{24,28},{28,20},{20,12},{12,4},{4,0},{1,9},{9... | collective-permute-start | bytes 1572872 | tf_op jit(solution)/shard_map/while/body/eval_jaxpr/ppermute | solution.py:69
  149.6 14.1 %collective-permute-start.1 = (bf16[256,1024]{1,0:T(8,128)(2,1)}, bf16[256,1024]{1,0:T(8,128)(2,1)}, u32[]{:S(2)}, u32[]{:S(2)}) collective-permute-start(bf16[256,1024]{1,0:T(8,128)(2,1)} %copy.17), channel_id=1, source_target_pairs={{8,0},{16,8},{24,16},{28,24},{20,28},{12,20},{4,12},{0,4},{9,1},{1... | collective-permute-start | bytes 1572872 | tf_op jit(solution)/shard_map/while/body/eval_jaxpr/ppermute | solution.py:70
  165.6 13.3 %collective-permute-start = (bf16[256,1024]{1,0:T(8,128)(2,1)}, bf16[256,1024]{1,0:T(8,128)(2,1)}, u32[]{:S(2)}, u32[]{:S(2)}) collective-permute-start(bf16[256,1024]{1,0:T(8,128)(2,1)} %copy.16), channel_id=1, source_target_pairs={{0,8},{8,16},{16,24},{24,28},{28,20},{20,12},{12,4},{4,0},{1,9},{9... | collective-permute-start | bytes 1572872 | tf_op jit(solution)/shard_map/while/body/eval_jaxpr/ppermute | solution.py:69
  169.0 13.0 %collective-permute-start.1 = (bf16[256,1024]{1,0:T(8,128)(2,1)}, bf16[256,1024]{1,0:T(8,128)(2,1)}, u32[]{:S(2)}, u32[]{:S(2)}) collective-permute-start(bf16[256,1024]{1,0:T(8,128)(2,1)} %copy.17), channel_id=1, source_target_pairs={{8,0},{16,8},{24,16},{28,24},{20,28},{12,20},{4,12},{0,4},{9,1},{1... | collective-permute-start | bytes 1572872 | tf_op jit(solution)/shard_map/while/body/eval_jaxpr/ppermute | solution.py:70
  183.8 13.3 %collective-permute-start = (bf16[256,1024]{1,0:T(8,128)(2,1)}, bf16[256,1024]{1,0:T(8,128)(2,1)}, u32[]{:S(2)}, u32[]{:S(2)}) collective-permute-start(bf16[256,1024]{1,0:T(8,128)(2,1)} %copy.16), channel_id=1, source_target_pairs={{0,8},{8,16},{16,24},{24,28},{28,20},{20,12},{12,4},{4,0},{1,9},{9... | collective-permute-start | bytes 1572872 | tf_op jit(solution)/shard_map/while/body/eval_jaxpr/ppermute | solution.py:69
  187.2 11.9 %collective-permute-start.1 = (bf16[256,1024]{1,0:T(8,128)(2,1)}, bf16[256,1024]{1,0:T(8,128)(2,1)}, u32[]{:S(2)}, u32[]{:S(2)}) collective-permute-start(bf16[256,1024]{1,0:T(8,128)(2,1)} %copy.17), channel_id=1, source_target_pairs={{8,0},{16,8},{24,16},{28,24},{20,28},{12,20},{4,12},{0,4},{9,1},{1... | collective-permute-start | bytes 1572872 | tf_op jit(solution)/shard_map/while/body/eval_jaxpr/ppermute | solution.py:70
  200.9 13.3 %collective-permute-start = (bf16[256,1024]{1,0:T(8,128)(2,1)}, bf16[256,1024]{1,0:T(8,128)(2,1)}, u32[]{:S(2)}, u32[]{:S(2)}) collective-permute-start(bf16[256,1024]{1,0:T(8,128)(2,1)} %copy.16), channel_id=1, source_target_pairs={{0,8},{8,16},{16,24},{24,28},{28,20},{20,12},{12,4},{4,0},{1,9},{9... | collective-permute-start | bytes 1572872 | tf_op jit(solution)/shard_map/while/body/eval_jaxpr/ppermute | solution.py:69
  204.2 10.7 %collective-permute-start.1 = (bf16[256,1024]{1,0:T(8,128)(2,1)}, bf16[256,1024]{1,0:T(8,128)(2,1)}, u32[]{:S(2)}, u32[]{:S(2)}) collective-permute-start(bf16[256,1024]{1,0:T(8,128)(2,1)} %copy.17), channel_id=1, source_target_pairs={{8,0},{16,8},{24,16},{28,24},{20,28},{12,20},{4,12},{0,4},{9,1},{1... | collective-permute-start | bytes 1572872 | tf_op jit(solution)/shard_map/while/body/eval_jaxpr/ppermute | solution.py:70
  216.8 13.3 %collective-permute-start = (bf16[256,1024]{1,0:T(8,128)(2,1)}, bf16[256,1024]{1,0:T(8,128)(2,1)}, u32[]{:S(2)}, u32[]{:S(2)}) collective-permute-start(bf16[256,1024]{1,0:T(8,128)(2,1)} %copy.16), channel_id=1, source_target_pairs={{0,8},{8,16},{16,24},{24,28},{28,20},{20,12},{12,4},{4,0},{1,9},{9... | collective-permute-start | bytes 1572872 | tf_op jit(solution)/shard_map/while/body/eval_jaxpr/ppermute | solution.py:69
  219.4 10.7 %collective-permute-start.1 = (bf16[256,1024]{1,0:T(8,128)(2,1)}, bf16[256,1024]{1,0:T(8,128)(2,1)}, u32[]{:S(2)}, u32[]{:S(2)}) collective-permute-start(bf16[256,1024]{1,0:T(8,128)(2,1)} %copy.17), channel_id=1, source_target_pairs={{8,0},{16,8},{24,16},{28,24},{20,28},{12,20},{4,12},{0,4},{9,1},{1... | collective-permute-start | bytes 1572872 | tf_op jit(solution)/shard_map/while/body/eval_jaxpr/ppermute | solution.py:70
  232.0 13.3 %collective-permute-start = (bf16[256,1024]{1,0:T(8,128)(2,1)}, bf16[256,1024]{1,0:T(8,128)(2,1)}, u32[]{:S(2)}, u32[]{:S(2)}) collective-permute-start(bf16[256,1024]{1,0:T(8,128)(2,1)} %copy.16), channel_id=1, source_target_pairs={{0,8},{8,16},{16,24},{24,28},{28,20},{20,12},{12,4},{4,0},{1,9},{9... | collective-permute-start | bytes 1572872 | tf_op jit(solution)/shard_map/while/body/eval_jaxpr/ppermute | solution.py:69
  234.6 10.7 %collective-permute-start.1 = (bf16[256,1024]{1,0:T(8,128)(2,1)}, bf16[256,1024]{1,0:T(8,128)(2,1)}, u32[]{:S(2)}, u32[]{:S(2)}) collective-permute-start(bf16[256,1024]{1,0:T(8,128)(2,1)} %copy.17), channel_id=1, source_target_pairs={{8,0},{16,8},{24,16},{28,24},{20,28},{12,20},{4,12},{0,4},{9,1},{1... | collective-permute-start | bytes 1572872 | tf_op jit(solution)/shard_map/while/body/eval_jaxpr/ppermute | solution.py:70
  355.7 9.4 %collective-permute-start.3 = (bf16[256,1024]{1,0:T(8,128)(2,1)}, bf16[256,1024]{1,0:T(8,128)(2,1)S(1)}, u32[]{:S(2)}, u32[]{:S(2)}) collective-permute-start(bf16[256,1024]{1,0:T(8,128)(2,1)} %convert_element_type.105), channel_id=1, source_target_pairs={{8,0},{16,8},{24,16},{28,24},{20,28},{12,20},{4,12},{0,4},{9,1},{1... | collective-permute-start | bytes 1572872 | tf_op jit(solution)/shard_map/while/body/eval_jaxpr/ppermute | solution.py:107
  358.5 9.3 %collective-permute-start.2 = (bf16[256,1024]{1,0:T(8,128)(2,1)S(1)}, bf16[256,1024]{1,0:T(8,128)(2,1)}, u32[]{:S(2)}, u32[]{:S(2)}) collective-permute-start(bf16[256,1024]{1,0:T(8,128)(2,1)S(1)} %convert_element_type.104), channel_id=1, source_target_pairs={{0,8},{8,16},{16,24},{24,28},{28,20},{20,12},{12,4},{4,0},{1,9},{9... | collective-permute-start | bytes 1572872 | tf_op jit(solution)/shard_map/while/body/eval_jaxpr/ppermute | solution.py:106
  371.4 9.4 %collective-permute-start.3 = (bf16[256,1024]{1,0:T(8,128)(2,1)}, bf16[256,1024]{1,0:T(8,128)(2,1)S(1)}, u32[]{:S(2)}, u32[]{:S(2)}) collective-permute-start(bf16[256,1024]{1,0:T(8,128)(2,1)} %convert_element_type.105), channel_id=1, source_target_pairs={{8,0},{16,8},{24,16},{28,24},{20,28},{12,20},{4,12},{0,4},{9,1},{1... | collective-permute-start | bytes 1572872 | tf_op jit(solution)/shard_map/while/body/eval_jaxpr/ppermute | solution.py:107
  374.1 9.4 %collective-permute-start.2 = (bf16[256,1024]{1,0:T(8,128)(2,1)S(1)}, bf16[256,1024]{1,0:T(8,128)(2,1)}, u32[]{:S(2)}, u32[]{:S(2)}) collective-permute-start(bf16[256,1024]{1,0:T(8,128)(2,1)S(1)} %convert_element_type.104), channel_id=1, source_target_pairs={{0,8},{8,16},{16,24},{24,28},{28,20},{20,12},{12,4},{4,0},{1,9},{9... | collective-permute-start | bytes 1572872 | tf_op jit(solution)/shard_map/while/body/eval_jaxpr/ppermute | solution.py:106
  387.1 10.5 %collective-permute-start.3 = (bf16[256,1024]{1,0:T(8,128)(2,1)}, bf16[256,1024]{1,0:T(8,128)(2,1)S(1)}, u32[]{:S(2)}, u32[]{:S(2)}) collective-permute-start(bf16[256,1024]{1,0:T(8,128)(2,1)} %convert_element_type.105), channel_id=1, source_target_pairs={{8,0},{16,8},{24,16},{28,24},{20,28},{12,20},{4,12},{0,4},{9,1},{1... | collective-permute-start | bytes 1572872 | tf_op jit(solution)/shard_map/while/body/eval_jaxpr/ppermute | solution.py:107
  389.7 10.6 %collective-permute-start.2 = (bf16[256,1024]{1,0:T(8,128)(2,1)S(1)}, bf16[256,1024]{1,0:T(8,128)(2,1)}, u32[]{:S(2)}, u32[]{:S(2)}) collective-permute-start(bf16[256,1024]{1,0:T(8,128)(2,1)S(1)} %convert_element_type.104), channel_id=1, source_target_pairs={{0,8},{8,16},{16,24},{24,28},{28,20},{20,12},{12,4},{4,0},{1,9},{9... | collective-permute-start | bytes 1572872 | tf_op jit(solution)/shard_map/while/body/eval_jaxpr/ppermute | solution.py:106
  403.8 12.0 %collective-permute-start.3 = (bf16[256,1024]{1,0:T(8,128)(2,1)}, bf16[256,1024]{1,0:T(8,128)(2,1)S(1)}, u32[]{:S(2)}, u32[]{:S(2)}) collective-permute-start(bf16[256,1024]{1,0:T(8,128)(2,1)} %convert_element_type.105), channel_id=1, source_target_pairs={{8,0},{16,8},{24,16},{28,24},{20,28},{12,20},{4,12},{0,4},{9,1},{1... | collective-permute-start | bytes 1572872 | tf_op jit(solution)/shard_map/while/body/eval_jaxpr/ppermute | solution.py:107
  407.4 12.4 %collective-permute-start.2 = (bf16[256,1024]{1,0:T(8,128)(2,1)S(1)}, bf16[256,1024]{1,0:T(8,128)(2,1)}, u32[]{:S(2)}, u32[]{:S(2)}) collective-permute-start(bf16[256,1024]{1,0:T(8,128)(2,1)S(1)} %convert_element_type.104), channel_id=1, source_target_pairs={{0,8},{8,16},{16,24},{24,28},{28,20},{20,12},{12,4},{4,0},{1,9},{9... | collective-permute-start | bytes 1572872 | tf_op jit(solution)/shard_map/while/body/eval_jaxpr/ppermute | solution.py:106
  423.4 13.6 %collective-permute-start.3 = (bf16[256,1024]{1,0:T(8,128)(2,1)}, bf16[256,1024]{1,0:T(8,128)(2,1)S(1)}, u32[]{:S(2)}, u32[]{:S(2)}) collective-permute-start(bf16[256,1024]{1,0:T(8,128)(2,1)} %convert_element_type.105), channel_id=1, source_target_pairs={{8,0},{16,8},{24,16},{28,24},{20,28},{12,20},{4,12},{0,4},{9,1},{1... | collective-permute-start | bytes 1572872 | tf_op jit(solution)/shard_map/while/body/eval_jaxpr/ppermute | solution.py:107
  425.7 13.8 %collective-permute-start.2 = (bf16[256,1024]{1,0:T(8,128)(2,1)S(1)}, bf16[256,1024]{1,0:T(8,128)(2,1)}, u32[]{:S(2)}, u32[]{:S(2)}) collective-permute-start(bf16[256,1024]{1,0:T(8,128)(2,1)S(1)} %convert_element_type.104), channel_id=1, source_target_pairs={{0,8},{8,16},{16,24},{24,28},{28,20},{20,12},{12,4},{4,0},{1,9},{9... | collective-permute-start | bytes 1572872 | tf_op jit(solution)/shard_map/while/body/eval_jaxpr/ppermute | solution.py:106
  443.2 14.3 %collective-permute-start.3 = (bf16[256,1024]{1,0:T(8,128)(2,1)}, bf16[256,1024]{1,0:T(8,128)(2,1)S(1)}, u32[]{:S(2)}, u32[]{:S(2)}) collective-permute-start(bf16[256,1024]{1,0:T(8,128)(2,1)} %convert_element_type.105), channel_id=1, source_target_pairs={{8,0},{16,8},{24,16},{28,24},{20,28},{12,20},{4,12},{0,4},{9,1},{1... | collective-permute-start | bytes 1572872 | tf_op jit(solution)/shard_map/while/body/eval_jaxpr/ppermute | solution.py:107
  445.2 14.8 %collective-permute-start.2 = (bf16[256,1024]{1,0:T(8,128)(2,1)S(1)}, bf16[256,1024]{1,0:T(8,128)(2,1)}, u32[]{:S(2)}, u32[]{:S(2)}) collective-permute-start(bf16[256,1024]{1,0:T(8,128)(2,1)S(1)} %convert_element_type.104), channel_id=1, source_target_pairs={{0,8},{8,16},{16,24},{24,28},{28,20},{20,12},{12,4},{4,0},{1,9},{9... | collective-permute-start | bytes 1572872 | tf_op jit(solution)/shard_map/while/body/eval_jaxpr/ppermute | solution.py:106
  463.7 9.4 %collective-permute-start.3 = (bf16[256,1024]{1,0:T(8,128)(2,1)}, bf16[256,1024]{1,0:T(8,128)(2,1)S(1)}, u32[]{:S(2)}, u32[]{:S(2)}) collective-permute-start(bf16[256,1024]{1,0:T(8,128)(2,1)} %convert_element_type.105), channel_id=1, source_target_pairs={{8,0},{16,8},{24,16},{28,24},{20,28},{12,20},{4,12},{0,4},{9,1},{1... | collective-permute-start | bytes 1572872 | tf_op jit(solution)/shard_map/while/body/eval_jaxpr/ppermute | solution.py:107
  465.5 10.2 %collective-permute-start.2 = (bf16[256,1024]{1,0:T(8,128)(2,1)S(1)}, bf16[256,1024]{1,0:T(8,128)(2,1)}, u32[]{:S(2)}, u32[]{:S(2)}) collective-permute-start(bf16[256,1024]{1,0:T(8,128)(2,1)S(1)} %convert_element_type.104), channel_id=1, source_target_pairs={{0,8},{8,16},{16,24},{24,28},{28,20},{20,12},{12,4},{4,0},{1,9},{9... | collective-permute-start | bytes 1572872 | tf_op jit(solution)/shard_map/while/body/eval_jaxpr/ppermute | solution.py:106
  (14 other events, 191.0 us)
Sparse Core Ops, SparseCore 0:
  11.4 51.7 all-gather.8
  64.8 56.8 all-gather.10
  250.6 42.9 all-gather.6
